TPU v7x, 256 devices: a whole 4x4x8 slice. The times are simulated.
256 devices in a mesh: seq: 64 (over y, z, core), tp: 4 (over x).
Axes of the slice: x: 4, y: 4, z: 8, core: 2. Of those that a mesh axis runs over, the one named last changes fastest.
Arguments:
- tokens: bfloat16 [512, 1152], P('seq'), may hold values from -6 to 6
- attn_gain: float32 [1152], replicated, may hold values from 0.1 to 1.9
- w_query: bfloat16 [1152, 1280], P(None, 'tp'), may hold values from -0.1875 to 0.1875
- w_key: bfloat16 [1152, 384], replicated, may hold values from -0.1875 to 0.1875
- w_value: bfloat16 [1152, 384], replicated, may hold values from -0.1875 to 0.1875
- w_out: bfloat16 [1280, 1152], P('tp'), may hold values from -0.1875 to 0.1875
- prefix_keys: bfloat16 [8, 32768, 384], P(None, 'seq'), may hold values from -92 to 92
- prefix_values: bfloat16 [8, 32768, 384], P(None, 'seq'), may hold values from -6 to 6
- suffix_keys: bfloat16 [512, 128, 384], P('seq'), may hold values from -92 to 92
- suffix_values: bfloat16 [512, 128, 384], P('seq'), may hold values from -6 to 6
- group_of: int32 [512], replicated, may hold values from 0 to 7, as said below
- prefix_len: int32 [8], replicated, may hold values from 1 to 32768, as said below
- suffix_len: int32 [512], replicated, may hold values from 0 to 128, as said below
- mlp_gain: float32 [1152], replicated, may hold values from 0.1 to 1.9
- w_gate: bfloat16 [1152, 3072], P(None, 'tp'), may hold values from -0.1875 to 0.1875
- w_up: bfloat16 [1152, 3072], P(None, 'tp'), may hold values from -0.1875 to 0.1875
- w_down: bfloat16 [3072, 1152], P('tp'), may hold values from -0.109375 to 0.109375
Outputs:
- layer_out: bfloat16 [512, 1152], P('seq')
Inputs may be any that keep to these rules, and one draw needn't show every extreme that they name: `group_of`: prompt group of each request; every request reads its group's stored prefix. `prefix_len`: stored prefix positions in use for each group. `suffix_len`: stored suffix positions in use for each request.
All inputs are finite; a program needn't handle non-finite values.
Results may differ from a plain program's by a relative error of at most 0.018.
Values may be sent and summed in bfloat16 or wider, within the bound.
No kernel may reach another device: no remote copies, remote signals or barrier semaphores. Data moves between devices by JAX's collectives and lax.ppermute only.
A program may use at most 192 MiB of HBM per device.

v0:
```python
import jax
import jax.numpy as jnp
from jax import lax
from jax.sharding import PartitionSpec as P

HEADS = 18
KV_HEADS = 6
HD = 64
NEG_FILL = -1e30


def rms_scale(values_in, gain_row):
    widened = values_in.astype(jnp.float32)
    factor = lax.rsqrt(jnp.mean(widened * widened, axis=-1, keepdims=True) + 1e-05)
    return (widened * factor * gain_row).astype(jnp.bfloat16)


def rotate_heads(blocks, position):
    half_dim = blocks.shape[-1] // 2
    frequency = jnp.power(10000.0, -jnp.arange(half_dim, dtype=jnp.float32) / half_dim)
    angles = position.astype(jnp.float32)[:, None, None] * frequency
    cosine = jnp.cos(angles)
    sine_part = jnp.sin(angles)
    low_half = blocks[..., :half_dim]
    high_half = blocks[..., half_dim:]
    return jnp.concatenate(
        [low_half * cosine - high_half * sine_part, high_half * cosine + low_half * sine_part],
        axis=-1,
    )


def slot_layout(device_tp, tp_count, slot_count):
    per_device = HEADS // tp_count
    surplus = HEADS % tp_count
    start_head = per_device * device_tp + jnp.minimum(device_tp, surplus)
    used_count = per_device + (device_tp < surplus).astype(jnp.int32)
    slot_ids = jnp.arange(slot_count, dtype=jnp.int32)
    head_ids = start_head + slot_ids
    slot_used = (slot_ids < used_count).astype(jnp.float32)
    kv_ids = jnp.minimum(head_ids, HEADS - 1) // (HEADS // KV_HEADS)
    return (kv_ids, slot_used)


def on_device(
    tokens,
    attn_gain,
    w_query,
    w_key,
    w_value,
    w_out,
    prefix_keys,
    prefix_values,
    suffix_keys,
    suffix_values,
    group_of,
    prefix_len,
    suffix_len,
    mlp_gain,
    w_gate,
    w_up,
    w_down,
):
    row_count = tokens.shape[0]
    slot_count = w_query.shape[1] // HD
    group_count = prefix_keys.shape[0]
    prefix_span = prefix_keys.shape[1]
    suffix_span = suffix_keys.shape[1]
    seq_index = lax.axis_index("seq")
    kv_ids, slot_used = slot_layout(lax.axis_index("tp"), lax.axis_size("tp"), slot_count)
    normed = rms_scale(tokens, attn_gain)
    queries = jnp.dot(normed, w_query, preferred_element_type=jnp.float32).reshape(
        row_count, slot_count, HD
    )
    new_keys = jnp.dot(normed, w_key, preferred_element_type=jnp.float32).reshape(
        row_count, KV_HEADS, HD
    )
    new_values = (
        jnp.dot(normed, w_value, preferred_element_type=jnp.float32)
        .astype(jnp.bfloat16)
        .reshape(row_count, KV_HEADS, HD)
    )
    own_start = seq_index * row_count
    own_groups = lax.dynamic_slice_in_dim(group_of, own_start, row_count)
    own_suffix = lax.dynamic_slice_in_dim(suffix_len, own_start, row_count)
    group_ids = jnp.arange(group_count, dtype=jnp.int32)
    own_prefix = jnp.sum(
        jnp.where(own_groups[:, None] == group_ids[None, :], prefix_len[None, :], 0), axis=1
    )
    position = own_prefix + own_suffix
    queries = rotate_heads(queries, position).astype(jnp.bfloat16)
    new_keys = rotate_heads(new_keys, position).astype(jnp.bfloat16)
    every_query = lax.all_gather(
        queries.reshape(row_count, slot_count * HD), "seq", axis=0, tiled=True
    )
    every_query = every_query.reshape(-1, slot_count, HD)
    request_count = every_query.shape[0]
    score_scale = HD ** (-0.5)
    pre_keys = jnp.take(prefix_keys.reshape(group_count, prefix_span, KV_HEADS, HD), kv_ids, axis=2)
    pre_values = jnp.take(
        prefix_values.reshape(group_count, prefix_span, KV_HEADS, HD), kv_ids, axis=2
    )
    pre_scores = (
        jnp.einsum("rsd,gpsd->rsgp", every_query, pre_keys, preferred_element_type=jnp.float32)
        * score_scale
    )
    pre_spots = seq_index * prefix_span + jnp.arange(prefix_span, dtype=jnp.int32)
    group_match = group_of[:, None] == group_ids[None, :]
    length_match = pre_spots[None, :] < prefix_len[:, None]
    pre_live = group_match[:, None, :, None] & length_match[None, None, :, :]
    top_score = jnp.max(
        jnp.where(pre_live, pre_scores, NEG_FILL).reshape(request_count, slot_count, -1), axis=2
    )
    pre_weights = jnp.where(pre_live, jnp.exp(pre_scores - top_score[:, :, None, None]), 0.0)
    totals = jnp.sum(pre_weights, axis=(2, 3))
    mixed_sum = jnp.einsum(
        "rsgp,gpsd->rsd",
        pre_weights.astype(jnp.bfloat16),
        pre_values,
        preferred_element_type=jnp.float32,
    )
    gathered = (
        lax.all_to_all(top_score[None], "seq", split_axis=1, concat_axis=0, tiled=True),
        lax.all_to_all(totals[None], "seq", split_axis=1, concat_axis=0, tiled=True),
        lax.all_to_all(mixed_sum[None], "seq", split_axis=1, concat_axis=0, tiled=True),
    )
    part_top = jnp.max(gathered[0], axis=0)
    part_scale = jnp.exp(gathered[0] - part_top[None])
    part_total = jnp.sum(part_scale * gathered[1], axis=0)
    part_mixed = jnp.sum(part_scale[..., None] * gathered[2], axis=0)
    suf_keys = jnp.take(suffix_keys.reshape(row_count, suffix_span, KV_HEADS, HD), kv_ids, axis=2)
    suf_values = jnp.take(
        suffix_values.reshape(row_count, suffix_span, KV_HEADS, HD), kv_ids, axis=2
    )
    suf_scores = (
        jnp.einsum("rsd,rjsd->rsj", queries, suf_keys, preferred_element_type=jnp.float32)
        * score_scale
    )
    suf_live = (jnp.arange(suffix_span, dtype=jnp.int32)[None, :] < own_suffix[:, None])[:, None, :]
    suf_top = jnp.max(jnp.where(suf_live, suf_scores, NEG_FILL), axis=2)
    own_keys = jnp.take(new_keys, kv_ids, axis=1).astype(jnp.float32)
    own_values = jnp.take(new_values, kv_ids, axis=1).astype(jnp.float32)
    own_score = jnp.sum(queries.astype(jnp.float32) * own_keys, axis=-1) * score_scale
    final_top = jnp.maximum(jnp.maximum(part_top, suf_top), own_score)
    carried = jnp.exp(part_top - final_top)
    suf_weights = jnp.where(suf_live, jnp.exp(suf_scores - final_top[:, :, None]), 0.0)
    own_weight = jnp.exp(own_score - final_top)
    denominator = carried * part_total + jnp.sum(suf_weights, axis=2) + own_weight
    own_low = lax.optimization_barrier(own_weight.astype(jnp.bfloat16)).astype(jnp.float32)
    numerator = carried[..., None] * part_mixed + own_low[..., None] * own_values
    numerator = numerator + jnp.einsum(
        "rsj,rjsd->rsd",
        suf_weights.astype(jnp.bfloat16),
        suf_values,
        preferred_element_type=jnp.float32,
    )
    attended = (numerator / denominator[..., None] * slot_used[None, :, None]).astype(jnp.bfloat16)
    head_part = jnp.dot(
        attended.reshape(row_count, slot_count * HD), w_out, preferred_element_type=jnp.float32
    )
    head_total = lax.psum(head_part.astype(jnp.bfloat16), "tp").astype(jnp.float32)
    hidden = (tokens.astype(jnp.float32) + head_total).astype(jnp.bfloat16)
    mlp_in = rms_scale(hidden, mlp_gain)
    gate_part = jnp.dot(mlp_in, w_gate, preferred_element_type=jnp.float32)
    up_part = jnp.dot(mlp_in, w_up, preferred_element_type=jnp.float32)
    activation = (jax.nn.silu(gate_part) * up_part).astype(jnp.bfloat16)
    down_part = jnp.dot(activation, w_down, preferred_element_type=jnp.float32)
    down_total = lax.psum(down_part.astype(jnp.bfloat16), "tp").astype(jnp.float32)
    return (hidden.astype(jnp.float32) + down_total).astype(jnp.bfloat16)


def solution(mesh):
    return jax.shard_map(
        on_device,
        mesh=mesh,
        in_specs=(
            P("seq", None),
            P(),
            P(None, "tp"),
            P(),
            P(),
            P("tp", None),
            P(None, "seq", None),
            P(None, "seq", None),
            P("seq", None, None),
            P("seq", None, None),
            P(),
            P(),
            P(),
            P(),
            P(None, "tp"),
            P(None, "tp"),
            P("tp", None),
        ),
        out_specs=P("seq", None),
        check_vma=False,
    )
```

profile of v0, /device:TPU:32, one launch (start us, length us, event | category | flops | bytes accessed | tf_op | source)
XLA Modules:
  0.0 266.4 jit_solution(10958488884695363522)
XLA Ops:
  9.7 50.4 %all_gather.3 = bf16[512,320]{1,0:T(8,128)(2,1)S(1)} all-gather(bf16[8,320]{1,0:T(8,128)(2,1)S(1)} %convert_element_type.88), channel_id=1, replica_groups=mesh['seq'=64,'tp'=4] {'seq'}, dimensions={0}, use_global_device_ids=true | all-gather | bytes 332800 | tf_op jit(solution)/shard_map/all_gather | solution.py:92
  60.3 4.7 %copy.81 = bf16[8,512,384]{1,2,0:T(8,128)(2,1)} copy(bf16[8,512,384]{2,1,0:T(8,128)(2,1)} %param.29) | data formatting | bytes 6291456 | tf_op args[6]
  65.0 3.9 %copy.82 = bf16[8,512,6,64]{1,3,0,2:T(8,128)(2,1)} copy(bf16[8,512,6,64]{1,3,2,0:T(8,128)(2,1)} %bitcast.92) | data formatting | bytes 6291456 | tf_op jit(solution)/shard_map/reshape | solution.py:98
  68.9 4.3 %gather_fusion = bf16[5,8,512,64]{2,3,1,0:T(8,128)(2,1)} fusion(bf16[8,512,6,64]{1,3,0,2:T(8,128)(2,1)} %copy.82, s32[1024]{0:T(1024)S(1)} %pad_clamp_fusion), kind=kCustom, calls=%fused_computation.clone | custom fusion | bytes 5242900 | tf_op jit(solution)/shard_map/jit(_take)/gather | solution.py:98
  75.2 19.6 %fusion = (f32[512,5]{0,1:T(8,128)S(1)}, f32[5,8,512,512]{3,2,1,0:T(8,128)}) fusion(pred[512,8,512]{0,2,1:T(8,128)(4,1)} %broadcast_and_fusion, bf16[512,5,64,1]{0,2,3,1:T(8,128)(2,1)S(1)} %bitcast.100, bf16[5,8,512,64]{2,3,1,0:T(8,128)(2,1)} %gather_fusion, pred[5]{0:T(512)(128)(4,1)S(1)} %get-tuple-element.36), kind=kOutput, calls=%fused_computation.8 | convolution fusion | flops 1374942720 | bytes 46999556 | tf_op jit(solution)/shard_map/rsd,gpsd->rsgp/dot_general | solution.py:103
  95.6 8.0 %all-to-all-start = ((f32[1,512,5]{2,0,1:T(1,128)}), f32[1,512,5]{2,0,1:T(1,128)S(1)}, u32[]{:S(2)}, u32[]{:S(2)}) async-start(f32[1,512,5]{2,0,1:T(1,128)} %copy.87), calls=%async_computation | async-start | bytes 524288 | tf_op jit(solution)/shard_map/all_to_all | solution.py:122
  105.9 2.3 copy.98
  110.0 4.7 %copy.92 = bf16[8,512,384]{1,2,0:T(8,128)(2,1)} copy(bf16[8,512,384]{2,1,0:T(8,128)(2,1)} %param.30) | data formatting | bytes 6291456 | tf_op args[7]
  114.7 3.9 %copy.93 = bf16[8,512,6,64]{1,3,0,2:T(8,128)(2,1)} copy(bf16[8,512,6,64]{1,3,2,0:T(8,128)(2,1)} %bitcast.93) | data formatting | bytes 6291456 | tf_op jit(solution)/shard_map/reshape | solution.py:100
  118.6 4.3 %gather_fusion.3 = bf16[5,8,512,64]{2,3,1,0:T(8,128)(2,1)} fusion(bf16[8,512,6,64]{1,3,0,2:T(8,128)(2,1)} %copy.93, s32[1024]{0:T(1024)S(1)} %pad_clamp_fusion), kind=kCustom, calls=%fused_computation.3.clone | custom fusion | bytes 5242900 | tf_op jit(solution)/shard_map/jit(_take)/gather | solution.py:99
  122.9 18.8 %fusion.3 = f32[512,5]{0,1:T(8,128)S(1)} fusion(f32[5,8,512,512]{3,2,1,0:T(8,128)} %get-tuple-element.35, f32[512,5]{0,1:T(8,128)S(1)} %get-tuple-element.34, pred[512,8,512]{0,2,1:T(8,128)(4,1)} %broadcast_and_fusion), kind=kLoop, calls=%fused_computation.11 | loop fusion | flops 41940480 | bytes 44060672 | tf_op jit(solution)/shard_map/reduce_sum | solution.py:114
  141.7 16.7 %fusion.18 = f32[1,512,5,64]{1,3,2,0:T(8,128)} fusion(f32[5,8,512,512]{3,2,1,0:T(8,128)} %get-tuple-element.35, f32[512,5]{0,1:T(8,128)S(1)} %get-tuple-element.34, pred[512,8,512]{0,2,1:T(8,128)(4,1)S(1)} %copy-done.2, bf16[5,8,512,64]{2,3,1,0:T(8,128)(2,1)S(1)} %copy-done.1, pred[5]{0:T(512)(128)(4,1)S(1)} %get-tuple-element.36), kind=kOutput, calls=%fused_computation.29 | convolution fusion | flops 1385431040 | bytes 47327236 | tf_op jit(solution)/shard_map/rsgp,gpsd->rsd/dot_general | solution.py:115
  160.9 10.5 %all-to-all-start.2 = ((f32[1,512,5]{2,0,1:T(1,128)}), f32[1,512,5]{2,0,1:T(1,128)}, u32[]{:S(2)}, u32[]{:S(2)}) async-start(f32[1,512,5]{2,0,1:T(1,128)} %copy.99), calls=%async_computation.2 | async-start | bytes 524288 | tf_op jit(solution)/shard_map/all_to_all | solution.py:123
  173.5 2.4 copy.95
  176.4 5.9 %reduce.1 = f32[512,5,64]{2,1,0:T(8,128)} reduce(f32[512,5,1,64]{3,2,1,0:T(1,128)S(1)} %bitcast.96, f32[]{:T(128)} %broadcast.335), dimensions={2}, to_apply=%bitcast.79.reduce_sub_computation | reduce | bytes 1310724
  182.4 3.1 %reshape.341 = f32[64,1,2560]{2,1,0:T(1,128)} reshape(f32[512,5,64]{2,1,0:T(8,128)} %reduce.1) | data formatting | bytes 1310720
  185.5 10.5 %all-to-all-start.1 = ((f32[64,1,2560]{2,1,0:T(1,128)}), f32[64,1,2560]{2,1,0:T(1,128)S(1)}, u32[]{:S(2)}, u32[]{:S(2)}) async-start(f32[64,1,2560]{2,1,0:T(1,128)} %reshape.341), calls=%async_computation.1 | async-start | bytes 1310720 | tf_op jit(solution)/shard_map/all_to_all | solution.py:124
  199.8 2.1 fusion.24
  201.9 14.0 %all-to-all-done.1 = f32[64,1,2560]{2,1,0:T(1,128)S(1)} async-done(((f32[64,1,2560]{2,1,0:T(1,128)}), f32[64,1,2560]{2,1,0:T(1,128)S(1)}, u32[]{:S(2)}, u32[]{:S(2)}) %all-to-all-start.1) | async-done | bytes 655392 | tf_op jit(solution)/shard_map/all_to_all | solution.py:124
  215.9 3.1 %reduce.2 = f32[64,2560]{1,0:T(8,128)} reduce(f32[64,1,2560]{2,1,0:T(1,128)S(1)} %all-to-all-done.1, f32[]{:T(128)} %broadcast.335), dimensions={1}, to_apply=%all_to_all.14.reduce_sub_computation | reduce | bytes 1310724 | tf_op jit(solution)/shard_map/all_to_all | solution.py:124
  219.1 2.7 %reshape.342 = f32[512,5,1,64]{3,2,1,0:T(1,128)S(1)} reshape(f32[64,2560]{1,0:T(8,128)} %reduce.2) | data formatting | bytes 1310720
  225.9 18.2 %psum.14 = bf16[8,1152]{1,0:T(8,128)(2,1)} all-reduce(bf16[8,1152]{1,0:T(8,128)(2,1)} %convolution_convert_fusion.1), channel_id=1, replica_groups=mesh['seq'=64,'tp'=4] {'tp'}, use_global_device_ids=true, to_apply=%region_10.14 | all-reduce | flops 9216 | bytes 36864 | tf_op jit(solution)/shard_map/psum | solution.py:160
  245.6 2.5 fusion.53
  250.2 14.9 %psum.15 = bf16[8,1152]{1,0:T(8,128)(2,1)S(1)} all-reduce(bf16[8,1152]{1,0:T(8,128)(2,1)} %convolution_convert_fusion), channel_id=1, replica_groups=mesh['seq'=64,'tp'=4] {'tp'}, use_global_device_ids=true, to_apply=%region_12.16 | all-reduce | flops 9216 | bytes 36864 | tf_op jit(solution)/shard_map/psum | solution.py:167
  (82 shorter events, 34.5 us)
Async XLA Ops:
  0.0 248.1 %copy-start = (bf16[768,1152]{1,0:T(8,128)(2,1)S(1)}, bf16[768,1152]{1,0:T(8,128)(2,1)}, u32[]{:S(2)}) copy-start(bf16[768,1152]{1,0:T(8,128)(2,1)} %param.39) | copy-start | bytes 5308420
  3.1 155.4 %copy-start.9 = (pred[5]{0:T(512)(128)(4,1)}, pred[5]{0:T(512)(128)(4,1)S(1)}, u32[]{:S(2)}) copy-start(pred[5]{0:T(512)(128)(4,1)S(1)} %get-tuple-element.36) | copy-start | bytes 19
  95.6 65.3 %all-to-all-start = ((f32[1,512,5]{2,0,1:T(1,128)}), f32[1,512,5]{2,0,1:T(1,128)S(1)}, u32[]{:S(2)}, u32[]{:S(2)}) async-start(f32[1,512,5]{2,0,1:T(1,128)} %copy.87), calls=%async_computation | async-start | bytes 524288 | tf_op jit(solution)/shard_map/all_to_all | solution.py:122
  122.9 18.8 %copy-start.1 = (bf16[5,8,512,64]{2,3,1,0:T(8,128)(2,1)S(1)}, bf16[5,8,512,64]{2,3,1,0:T(8,128)(2,1)}, u32[]{:S(2)}) copy-start(bf16[5,8,512,64]{2,3,1,0:T(8,128)(2,1)} %gather_fusion.3) | copy-start | bytes 7864324
  122.9 18.8 %copy-start.2 = (pred[512,8,512]{0,2,1:T(8,128)(4,1)S(1)}, pred[512,8,512]{0,2,1:T(8,128)(4,1)}, u32[]{:S(2)}) copy-start(pred[512,8,512]{0,2,1:T(8,128)(4,1)} %broadcast_and_fusion) | copy-start | bytes 6291460
  158.4 1.3 copy-start.4
  158.5 1.3 copy-start.5
  158.5 1.3 copy-start.7
  160.9 24.6 %all-to-all-start.2 = ((f32[1,512,5]{2,0,1:T(1,128)}), f32[1,512,5]{2,0,1:T(1,128)}, u32[]{:S(2)}, u32[]{:S(2)}) async-start(f32[1,512,5]{2,0,1:T(1,128)} %copy.99), calls=%async_computation.2 | async-start | bytes 524288 | tf_op jit(solution)/shard_map/all_to_all | solution.py:123
  185.5 30.5 %all-to-all-start.1 = ((f32[64,1,2560]{2,1,0:T(1,128)}), f32[64,1,2560]{2,1,0:T(1,128)S(1)}, u32[]{:S(2)}, u32[]{:S(2)}) async-start(f32[64,1,2560]{2,1,0:T(1,128)} %reshape.341), calls=%async_computation.1 | async-start | bytes 1310720 | tf_op jit(solution)/shard_map/all_to_all | solution.py:124
  222.2 25.8 %copy-start.3 = (bf16[1152,768]{1,0:T(8,128)(2,1)S(1)}, bf16[1152,768]{1,0:T(8,128)(2,1)}, u32[]{:S(2)}) copy-start(bf16[1152,768]{1,0:T(8,128)(2,1)} %param.38) | copy-start | bytes 5308420
  223.9 24.2 %copy-start.8 = (f32[1152]{0:T(1024)S(1)}, f32[1152]{0:T(1024)}, u32[]{:S(2)}) copy-start(f32[1152]{0:T(1024)} %param.36) | copy-start | bytes 13828
  245.0 0.6 copy-start.6
where the time goes:
time: 268 us; the launch traced here: 266 us
  blocking collectives  83.5 us (31%)
  matrix products  49.5 us (18%)
  local copies, waits for them, and re-layouts  48.6 us (18%)
  other arithmetic  41.5 us (15%)
  starting transfers between devices  29.1 us (11%)
  waiting for transfers between devices  14 us (5%)
    all_gather x1, blocking collectives, on_device(): lax.all_gather(queries.reshape(row_count, slot_count * HD), 'seq', axis=0...  50.4 us
    unnamed x28, local copies, waits for them, and re-layouts  20.3 us
    dot_general x1, matrix products, on_device(): jnp.einsum('rsd,gpsd->rsgp', every_query, pre_keys, preferred_element_typ...  19.6 us
    reduce_sum x1, other arithmetic, on_device(): totals = jnp.sum(pre_weights, axis=(2, 3))  18.8 us
    psum x1, blocking collectives, on_device(): lax.psum(head_part.astype(jnp.bfloat16), 'tp').astype(jnp.float32)  18.2 us
    dot_general x1, matrix products, on_device(): jnp.einsum('rsgp,gpsd->rsd', pre_weights.astype(jnp.bfloat16), pre_values...  16.7 us
    psum x1, blocking collectives, on_device(): lax.psum(down_part.astype(jnp.bfloat16), 'tp').astype(jnp.float32)  14.9 us
    all_to_all x1, waiting for transfers between devices, on_device(): lax.all_to_all(mixed_sum[None], 'seq', split_axis=1, concat_axis=0, tiled...  14 us
  transfers between devices with their start and end apart: 3, of which 1 were waited for; matrix products, arithmetic and copies ran while one was open for 29% of the time, Pallas kernels for 0%

commit v1 on v0

--- a/solution.py
+++ b/solution.py
@@ -120,7 +120,12 @@
     )
     gathered = (
         lax.all_to_all(top_score[None], "seq", split_axis=1, concat_axis=0, tiled=True),
-        lax.all_to_all(totals[None], "seq", split_axis=1, concat_axis=0, tiled=True),
+        jnp.concatenate(
+            lax.all_to_all(
+                jnp.stack(jnp.split(totals[None], lax.axis_size("seq"), axis=1)), "seq", 0, 0
+            ),
+            axis=0,
+        ),
         lax.all_to_all(mixed_sum[None], "seq", split_axis=1, concat_axis=0, tiled=True),
     )
     part_top = jnp.max(gathered[0], axis=0)

time: 268 us -> 270 us (level)
    unnamed x28 -> x36, local copies, waits for them, and re-layouts: 20.3 us -> 20.2 us
  transfers between devices with their start and end apart: 3 -> 3, of which waited for: 1 -> 1; matrix products, arithmetic and copies ran while one was open for 29% -> 22% of each run, Pallas kernels for 0% -> 0%
where the time goes in v1:
time: 270 us; the launch traced here: 269 us
  blocking collectives  83.5 us (31%)
  matrix products  51.6 us (19%)
  local copies, waits for them, and re-layouts  48.1 us (18%)
  other arithmetic  41 us (15%)
  starting transfers between devices  28.7 us (11%)
  waiting for transfers between devices  15.4 us (6%)
    all_gather x1, blocking collectives, on_device(): lax.all_gather(queries.reshape(row_count, slot_count * HD), 'seq', axis=0...  50.4 us
    unnamed x36, local copies, waits for them, and re-layouts  20.2 us
    dot_general x1, matrix products, on_device(): jnp.einsum('rsd,gpsd->rsgp', every_query, pre_keys, preferred_element_typ...  19.6 us
    dot_general x1, matrix products, on_device(): jnp.einsum('rsgp,gpsd->rsd', pre_weights.astype(jnp.bfloat16), pre_values...  18.8 us
    psum x1, blocking collectives, on_device(): lax.psum(head_part.astype(jnp.bfloat16), 'tp').astype(jnp.float32)  18.2 us
    reduce_sum x1, other arithmetic, on_device(): totals = jnp.sum(pre_weights, axis=(2, 3))  18.1 us
    all_to_all x1, waiting for transfers between devices, on_device(): lax.all_to_all(mixed_sum[None], 'seq', split_axis=1, concat_axis=0, tiled...  15.4 us
    psum x1, blocking collectives, on_device(): lax.psum(down_part.astype(jnp.bfloat16), 'tp').astype(jnp.float32)  14.9 us
  transfers between devices with their start and end apart: 3, of which 1 were waited for; matrix products, arithmetic and copies ran while one was open for 22% of the time, Pallas kernels for 0%

profile of v1, /device:TPU:32, one launch (start us, length us, event | category | flops | bytes accessed | tf_op | source)
XLA Modules:
  0.0 268.7 jit_solution(12710181129257673156)
XLA Ops:
  10.2 50.4 %all_gather.3 = bf16[512,320]{1,0:T(8,128)(2,1)S(1)} all-gather(bf16[8,320]{1,0:T(8,128)(2,1)S(1)} %convert_element_type.88), channel_id=1, replica_groups=mesh['seq'=64,'tp'=4] {'seq'}, dimensions={0}, use_global_device_ids=true | all-gather | bytes 332800 | tf_op jit(solution)/shard_map/all_gather | solution.py:92
  60.7 4.7 %copy.213 = bf16[8,512,384]{1,2,0:T(8,128)(2,1)} copy(bf16[8,512,384]{2,1,0:T(8,128)(2,1)} %param.29) | data formatting | bytes 6291456 | tf_op args[6]
  65.4 3.9 %copy.214 = bf16[8,512,6,64]{1,3,0,2:T(8,128)(2,1)} copy(bf16[8,512,6,64]{1,3,2,0:T(8,128)(2,1)} %bitcast.224) | data formatting | bytes 6291456 | tf_op jit(solution)/shard_map/reshape | solution.py:98
  69.3 4.3 %gather_fusion = bf16[5,8,512,64]{2,3,1,0:T(8,128)(2,1)} fusion(bf16[8,512,6,64]{1,3,0,2:T(8,128)(2,1)} %copy.214, s32[1024]{0:T(1024)S(1)} %pad_clamp_fusion), kind=kCustom, calls=%fused_computation.clone | custom fusion | bytes 5242900 | tf_op jit(solution)/shard_map/jit(_take)/gather | solution.py:98
  75.6 19.6 %fusion = (f32[512,5]{0,1:T(8,128)S(1)}, f32[5,8,512,512]{3,2,1,0:T(8,128)}) fusion(pred[512,8,512]{0,2,1:T(8,128)(4,1)} %broadcast_and_fusion, bf16[512,5,64,1]{0,2,3,1:T(8,128)(2,1)S(1)} %bitcast.232, bf16[5,8,512,64]{2,3,1,0:T(8,128)(2,1)} %gather_fusion, pred[5]{0:T(512)(128)(4,1)S(1)} %get-tuple-element.100), kind=kOutput, calls=%fused_computation.8 | convolution fusion | flops 1374942720 | bytes 46999556 | tf_op jit(solution)/shard_map/rsd,gpsd->rsgp/dot_general | solution.py:103
  95.2 18.1 %fusion.3 = f32[512,5]{0,1:T(8,128)S(1)} fusion(f32[5,8,512,512]{3,2,1,0:T(8,128)} %get-tuple-element.99, f32[512,5]{0,1:T(8,128)S(1)} %get-tuple-element.98, pred[512,8,512]{0,2,1:T(8,128)(4,1)} %broadcast_and_fusion), kind=kLoop, calls=%fused_computation.11 | loop fusion | flops 41940480 | bytes 44060672 | tf_op jit(solution)/shard_map/reduce_sum | solution.py:114
  115.1 8.0 %all-to-all-start.2 = ((f32[64,1,8,5]{2,1,3,0:T(1,128)}), f32[64,1,8,5]{2,1,3,0:T(1,128)S(1)}, u32[]{:S(2)}, u32[]{:S(2)}) async-start(f32[64,1,8,5]{2,1,3,0:T(1,128)} %copy.231), calls=%async_computation.2 | async-start | bytes 327680 | tf_op jit(solution)/shard_map/all_to_all | solution.py:124
  125.3 2.3 copy.230
  129.5 4.7 %copy.224 = bf16[8,512,384]{1,2,0:T(8,128)(2,1)} copy(bf16[8,512,384]{2,1,0:T(8,128)(2,1)} %param.30) | data formatting | bytes 6291456 | tf_op args[7]
  134.1 3.9 %copy.225 = bf16[8,512,6,64]{1,3,0,2:T(8,128)(2,1)} copy(bf16[8,512,6,64]{1,3,2,0:T(8,128)(2,1)} %bitcast.225) | data formatting | bytes 6291456 | tf_op jit(solution)/shard_map/reshape | solution.py:100
  138.1 4.3 %gather_fusion.3 = bf16[5,8,512,64]{2,3,1,0:T(8,128)(2,1)} fusion(bf16[8,512,6,64]{1,3,0,2:T(8,128)(2,1)} %copy.225, s32[1024]{0:T(1024)S(1)} %pad_clamp_fusion), kind=kCustom, calls=%fused_computation.3.clone | custom fusion | bytes 5242900 | tf_op jit(solution)/shard_map/jit(_take)/gather | solution.py:99
  142.4 18.8 %fusion.18 = f32[1,512,5,64]{1,3,2,0:T(8,128)} fusion(f32[5,8,512,512]{3,2,1,0:T(8,128)} %get-tuple-element.99, f32[512,5]{0,1:T(8,128)S(1)} %get-tuple-element.98, pred[512,8,512]{0,2,1:T(8,128)(4,1)} %broadcast_and_fusion, bf16[5,8,512,64]{2,3,1,0:T(8,128)(2,1)} %gather_fusion.3, pred[5]{0:T(512)(128)(4,1)S(1)} %copy-done.10), kind=kOutput, calls=%fused_computation.29 | convolution fusion | flops 1385431040 | bytes 47327236 | tf_op jit(solution)/shard_map/rsgp,gpsd->rsd/dot_general | solution.py:115
  163.6 10.3 %all-to-all-start = ((f32[1,512,5]{2,0,1:T(1,128)}), f32[1,512,5]{2,0,1:T(1,128)S(1)}, u32[]{:S(2)}, u32[]{:S(2)}) async-start(f32[1,512,5]{2,0,1:T(1,128)} %copy.219), calls=%async_computation | async-start | bytes 524288 | tf_op jit(solution)/shard_map/all_to_all | solution.py:122
  176.1 2.4 copy.227
  179.0 5.9 %reduce.1 = f32[512,5,64]{2,1,0:T(8,128)} reduce(f32[512,5,1,64]{3,2,1,0:T(1,128)S(1)} %bitcast.228, f32[]{:T(128)} %broadcast.329), dimensions={2}, to_apply=%bitcast.211.reduce_sub_computation | reduce | bytes 1310724
  184.9 3.1 %reshape.339 = f32[64,1,2560]{2,1,0:T(1,128)} reshape(f32[512,5,64]{2,1,0:T(8,128)} %reduce.1) | data formatting | bytes 1310720
  188.0 10.3 %all-to-all-start.1 = ((f32[64,1,2560]{2,1,0:T(1,128)}), f32[64,1,2560]{2,1,0:T(1,128)S(1)}, u32[]{:S(2)}, u32[]{:S(2)}) async-start(f32[64,1,2560]{2,1,0:T(1,128)} %reshape.339), calls=%async_computation.1 | async-start | bytes 1310720 | tf_op jit(solution)/shard_map/all_to_all | solution.py:129
  200.6 2.1 fusion.24
  202.8 15.4 %all-to-all-done.1 = f32[64,1,2560]{2,1,0:T(1,128)S(1)} async-done(((f32[64,1,2560]{2,1,0:T(1,128)}), f32[64,1,2560]{2,1,0:T(1,128)S(1)}, u32[]{:S(2)}, u32[]{:S(2)}) %all-to-all-start.1) | async-done | bytes 655392 | tf_op jit(solution)/shard_map/all_to_all | solution.py:129
  218.2 3.1 %reduce.2 = f32[64,2560]{1,0:T(8,128)} reduce(f32[64,1,2560]{2,1,0:T(1,128)S(1)} %all-to-all-done.1, f32[]{:T(128)} %broadcast.329), dimensions={1}, to_apply=%all_to_all.23.reduce_sub_computation | reduce | bytes 1310724 | tf_op jit(solution)/shard_map/all_to_all | solution.py:129
  221.3 2.7 %reshape.340 = f32[512,5,1,64]{3,2,1,0:T(1,128)S(1)} reshape(f32[64,2560]{1,0:T(8,128)} %reduce.2) | data formatting | bytes 1310720
  228.1 18.2 %psum.14 = bf16[8,1152]{1,0:T(8,128)(2,1)} all-reduce(bf16[8,1152]{1,0:T(8,128)(2,1)} %convolution_convert_fusion.1), channel_id=1, replica_groups=mesh['seq'=64,'tp'=4] {'tp'}, use_global_device_ids=true, to_apply=%region_10.14 | all-reduce | flops 9216 | bytes 36864 | tf_op jit(solution)/shard_map/psum | solution.py:165
  247.8 2.5 fusion.54
  252.4 14.9 %psum.15 = bf16[8,1152]{1,0:T(8,128)(2,1)S(1)} all-reduce(bf16[8,1152]{1,0:T(8,128)(2,1)} %convolution_convert_fusion), channel_id=1, replica_groups=mesh['seq'=64,'tp'=4] {'tp'}, use_global_device_ids=true, to_apply=%region_12.16 | all-reduce | flops 9216 | bytes 36864 | tf_op jit(solution)/shard_map/psum | solution.py:172
  (95 shorter events, 34.4 us)
Async XLA Ops:
  0.0 250.3 %copy-start = (bf16[768,1152]{1,0:T(8,128)(2,1)S(1)}, bf16[768,1152]{1,0:T(8,128)(2,1)}, u32[]{:S(2)}) copy-start(bf16[768,1152]{1,0:T(8,128)(2,1)} %param.39) | copy-start | bytes 5308420
  2.4 5.1 %copy-start.11 = (f32[8]{0:T(128)}, f32[8]{0:T(128)S(1)}, u32[]{:S(2)}) copy-start(f32[8]{0:T(128)S(1)} %add_rsqrt_fusion.1) | copy-start | bytes 100
  3.0 72.6 %copy-start.9 = (pred[5]{0:T(512)(128)(4,1)}, pred[5]{0:T(512)(128)(4,1)S(1)}, u32[]{:S(2)}) copy-start(pred[5]{0:T(512)(128)(4,1)S(1)} %get-tuple-element.100) | copy-start | bytes 19
  4.6 133.5 %copy-start.8 = (s32[1024]{0:T(1024)}, s32[1024]{0:T(1024)S(1)}, u32[]{:S(2)}) copy-start(s32[1024]{0:T(1024)S(1)} %pad_clamp_fusion) | copy-start | bytes 12292
  115.1 48.5 %all-to-all-start.2 = ((f32[64,1,8,5]{2,1,3,0:T(1,128)}), f32[64,1,8,5]{2,1,3,0:T(1,128)S(1)}, u32[]{:S(2)}, u32[]{:S(2)}) async-start(f32[64,1,8,5]{2,1,3,0:T(1,128)} %copy.231), calls=%async_computation.2 | async-start | bytes 327680 | tf_op jit(solution)/shard_map/all_to_all | solution.py:124
  138.0 4.3 %copy-start.10 = (pred[5]{0:T(512)(128)(4,1)S(1)}, pred[5]{0:T(512)(128)(4,1)}, u32[]{:S(2)}) copy-start(pred[5]{0:T(512)(128)(4,1)} %copy-done.9) | copy-start | bytes 19
  161.1 1.3 copy-start.2
  161.1 1.3 copy-start.3
  161.1 1.3 copy-start.5
  161.2 1.3 copy-start.12
  163.6 24.4 %all-to-all-start = ((f32[1,512,5]{2,0,1:T(1,128)}), f32[1,512,5]{2,0,1:T(1,128)S(1)}, u32[]{:S(2)}, u32[]{:S(2)}) async-start(f32[1,512,5]{2,0,1:T(1,128)} %copy.219), calls=%async_computation | async-start | bytes 524288 | tf_op jit(solution)/shard_map/all_to_all | solution.py:122
  184.9 13.4 %copy-start.13 = (s32[8]{0:T(128)S(1)}, s32[8]{0:T(128)}, u32[]{:S(2)}) copy-start(s32[8]{0:T(128)} %get-tuple-element.19) | copy-start | bytes 100
  188.0 30.2 %all-to-all-start.1 = ((f32[64,1,2560]{2,1,0:T(1,128)}), f32[64,1,2560]{2,1,0:T(1,128)S(1)}, u32[]{:S(2)}, u32[]{:S(2)}) async-start(f32[64,1,2560]{2,1,0:T(1,128)} %reshape.339), calls=%async_computation.1 | async-start | bytes 1310720 | tf_op jit(solution)/shard_map/all_to_all | solution.py:129
  200.6 23.8 %copy-start.7 = (f32[8,5]{0,1:T(8,128)S(1)}, f32[8,5]{0,1:T(8,128)}, u32[]{:S(2)}) copy-start(f32[8,5]{0,1:T(8,128)} %get-tuple-element.12) | copy-start | bytes 484
  224.4 25.8 %copy-start.1 = (bf16[1152,768]{1,0:T(8,128)(2,1)S(1)}, bf16[1152,768]{1,0:T(8,128)(2,1)}, u32[]{:S(2)}) copy-start(bf16[1152,768]{1,0:T(8,128)(2,1)} %param.38) | copy-start | bytes 5308420
  226.1 24.2 %copy-start.6 = (f32[1152]{0:T(1024)S(1)}, f32[1152]{0:T(1024)}, u32[]{:S(2)}) copy-start(f32[1152]{0:T(1024)} %param.36) | copy-start | bytes 13828
  247.2 0.6 copy-start.4
